TPU v7x, 256 devices: a whole 4x4x8 slice. The times are simulated.
256 devices in a mesh: dp: 8 (over y_hi, x), seq: 16 (over y_lo, z), segment: 2 (over core).
Axes of the slice: x: 4, y: 4 (y_hi: 2, y_lo: 2; y = y_hi * 2 + y_lo), z: 8, core: 2. Of those that a mesh axis runs over, the one named last changes fastest.
Arguments:
- saved_input: bfloat16 [2, 8, 8192, 256], P('segment', 'dp', 'seq'), may hold values from -6 to 6
- upstream: bfloat16 [8, 8192, 256], P('dp', 'seq'), may hold values from -6 to 6
- clip_lengths: int32 [8, 32], P('dp'), may hold values from 1 to 2048, 8192 in all within a row
- conv_a: bfloat16 [2, 3, 7, 256, 256], P('segment'), may hold values from -0.125 to 0.125
- bias_a: float32 [2, 3, 256], P('segment'), may hold values from -3 to 3
- conv_b: bfloat16 [2, 3, 256, 256], P('segment'), may hold values from -0.375 to 0.375
Outputs:
- section_input_grad: bfloat16 [2, 8, 8192, 256], P('segment', 'dp', 'seq')
- grad_conv_a: float32 [2, 3, 7, 256, 256], P('segment')
- grad_bias_a: float32 [2, 3, 256], P('segment')
- grad_conv_b: float32 [2, 3, 256, 256], P('segment')
Inputs may be any that keep to these rules, and one draw needn't show every extreme that they name: `clip_lengths`: each row's 32 lengths sum to 8192, and the longest is exactly 2048.
All inputs are finite; a program needn't handle non-finite values.
Results may differ from a plain program's by a relative error of at most 0.02.
Values may be sent and summed in bfloat16 or wider, within the bound.
No kernel may reach another device: no remote copies, remote signals or barrier semaphores. Data moves between devices by JAX's collectives and lax.ppermute only.
A program may use at most 128 MiB of HBM per device.

v0:
```python
import jax
import jax.numpy as jnp
from jax import lax
from jax.sharding import PartitionSpec as P

KERNEL = 7
UNITS = 3


def with_halo(cells, sides, width):
    for axis, dim in sides:
        count = lax.axis_size(axis)
        ends = count - 1
        head = lax.slice_in_dim(cells, 0, width, axis=dim)
        tail = lax.slice_in_dim(cells, cells.shape[dim] - width, cells.shape[dim], axis=dim)
        cells = jnp.concatenate(
            [
                lax.ppermute(tail, axis, [(i, (i + 1) % count) for i in range(ends)]),
                cells,
                lax.ppermute(head, axis, [((i + 1) % count, i) for i in range(ends)]),
            ],
            axis=dim,
        )
    return cells


def spread(value, axis, root):
    mine = lax.axis_index(axis) == root
    return lax.psum(jnp.where(mine, value, jnp.zeros_like(value)), axis)


def elu_act(value):
    return jnp.where(value > 0, value, jnp.expm1(jnp.minimum(value, 0.0)))


def elu_slope(value):
    return jnp.where(value > 0, 1.0, jnp.exp(jnp.minimum(value, 0.0)))


def spread_acts(active, reach):
    return with_halo(active, (("seq", 0),), reach)


def spread_grads(gate, reach):
    return with_halo(gate, (("seq", 0),), reach)


def shards(saved_input, upstream, clip_lengths, conv_a, bias_a, conv_b):
    stream = saved_input[0, 0]
    lengths = clip_lengths[0]
    weights_a = conv_a[0]
    biases_a = bias_a[0]
    weights_b = conv_b[0]
    frames = stream.shape[0]
    channels = stream.shape[1]
    inner = weights_a.shape[3]
    half = KERNEL // 2
    furthest = half * 3 ** (UNITS - 1)
    offset = lax.axis_index("seq") * frames
    is_decoder = lax.axis_index("segment") == 1
    clip_ends = jnp.cumsum(lengths)
    places = offset - furthest + jnp.arange(frames + 2 * furthest, dtype=jnp.int32)
    clip_of = jnp.sum((places[:, None] >= clip_ends[None, :]).astype(jnp.int32), axis=1)
    own_clip = clip_of[furthest : furthest + frames]

    def linked(shift_by):
        return (clip_of[furthest + shift_by : furthest + shift_by + frames] == own_clip)[:, None]

    stored = []
    for unit_idx in range(UNITS):
        dilation = 3**unit_idx
        reach = half * dilation
        active = elu_act(stream.astype(jnp.float32)).astype(jnp.bfloat16)
        padded = spread_acts(active, reach)
        tap_rows = jnp.concatenate(
            [
                jnp.where(
                    linked((tap_no - half) * dilation),
                    padded[
                        reach
                        + (tap_no - half) * dilation : reach
                        + (tap_no - half) * dilation
                        + frames
                    ],
                    jnp.zeros((), jnp.bfloat16),
                )
                for tap_no in range(KERNEL)
            ],
            axis=1,
        )
        pre_act = biases_a[unit_idx][None, :] + jnp.dot(
            tap_rows,
            weights_a[unit_idx].reshape(KERNEL * channels, inner),
            preferred_element_type=jnp.float32,
        )
        squashed = elu_act(pre_act).astype(jnp.bfloat16)
        next_stream = (
            stream.astype(jnp.float32)
            + jnp.dot(squashed, weights_b[unit_idx], preferred_element_type=jnp.float32)
        ).astype(jnp.bfloat16)
        stored.append((stream, tap_rows, pre_act, squashed))
        stream = next_stream

    def unit_back(unit_idx, grad_y):
        dilation = 3**unit_idx
        reach = half * dilation
        stream_in, tap_rows, pre_act, squashed = stored[unit_idx]
        grad_b = lax.dot_general(
            grad_y,
            weights_b[unit_idx],
            (((1,), (1,)), ((), ())),
            preferred_element_type=jnp.float32,
        )
        gate = (grad_b * elu_slope(pre_act)).astype(jnp.bfloat16)
        gate_padded = spread_grads(gate, reach)
        back_rows = jnp.concatenate(
            [
                jnp.where(
                    linked(-(tap_no - half) * dilation),
                    gate_padded[
                        reach
                        - (tap_no - half) * dilation : reach
                        - (tap_no - half) * dilation
                        + frames
                    ],
                    jnp.zeros((), jnp.bfloat16),
                )
                for tap_no in range(KERNEL)
            ],
            axis=1,
        )
        turned = jnp.transpose(weights_a[unit_idx], (0, 2, 1)).reshape(KERNEL * inner, channels)
        back = jnp.dot(back_rows, turned, preferred_element_type=jnp.float32)
        grad_next = (
            grad_y.astype(jnp.float32) + back * elu_slope(stream_in.astype(jnp.float32))
        ).astype(jnp.bfloat16)
        return (gate, grad_next)

    first_gates = [None] * UNITS
    first_grads = [None] * (UNITS + 1)
    grad_y = upstream[0]
    first_grads[UNITS] = grad_y
    for unit_idx in reversed(range(UNITS)):
        gate, grad_y = unit_back(unit_idx, grad_y)
        first_gates[unit_idx] = gate
        first_grads[unit_idx] = grad_y
    latent = lax.ppermute(grad_y, "segment", [(1, 0)])
    grads_a = [None] * UNITS
    grads_bias = [None] * UNITS
    grads_b = [None] * UNITS
    contract = (((0,), (0,)), ((), ()))
    grad_y = latent
    for unit_idx in reversed(range(UNITS)):
        stream_in, tap_rows, pre_act, squashed = stored[unit_idx]
        gate_two, grad_next = unit_back(unit_idx, grad_y)
        gate = jnp.where(is_decoder, first_gates[unit_idx], gate_two)
        grad_out = jnp.where(is_decoder, first_grads[unit_idx + 1], grad_y)
        unit_b = lax.dot_general(squashed, grad_out, contract, preferred_element_type=jnp.float32)
        unit_bias = jnp.sum(gate.astype(jnp.float32), axis=0)
        unit_a = lax.dot_general(
            tap_rows, gate, contract, preferred_element_type=jnp.float32
        ).reshape(KERNEL, channels, inner)
        grads_a[unit_idx] = unit_a
        grads_bias[unit_idx] = unit_bias
        grads_b[unit_idx] = unit_b
        grad_y = grad_next
    section_grad = jnp.where(is_decoder, first_grads[0], grad_y)
    rows_a = UNITS * KERNEL * channels
    rows_b = UNITS * inner
    packed = jnp.concatenate(
        [
            jnp.stack(grads_a).reshape(rows_a, inner),
            jnp.stack(grads_b).reshape(rows_b, channels),
            jnp.pad(jnp.stack(grads_bias), ((0, 8 - UNITS), (0, 0))),
        ],
        axis=0,
    )
    group = lax.axis_size("dp") * lax.axis_size("seq")
    rows = packed.shape[0]
    share = -(-rows // (group * 8)) * 8
    packed = jnp.pad(packed, ((0, share * group - rows), (0, 0)))
    packed = lax.psum_scatter(packed, ("dp", "seq"), scatter_dimension=0, tiled=True)
    packed = lax.all_gather(packed.astype(jnp.bfloat16), ("dp", "seq"), axis=0, tiled=True).astype(
        jnp.float32
    )
    total_a = packed[:rows_a].reshape(UNITS, KERNEL, channels, inner)
    total_b = packed[rows_a : rows_a + rows_b].reshape(UNITS, inner, channels)
    total_bias = packed[rows_a + rows_b : rows_a + rows_b + UNITS]
    return (section_grad[None, None], total_a[None], total_bias[None], total_b[None])


def solution(mesh):
    placed = (
        P("segment", "dp", "seq", None),
        P("dp", "seq", None),
        P("dp", None),
        P("segment", None, None, None, None),
        P("segment", None, None),
        P("segment", None, None, None),
    )
    return jax.shard_map(
        shards,
        mesh=mesh,
        in_specs=placed,
        out_specs=(
            P("segment", "dp", "seq", None),
            P("segment", None, None, None, None),
            P("segment", None, None),
            P("segment", None, None, None),
        ),
        check_vma=False,
    )
```

profile of v0, /device:TPU:0, one launch (start us, length us, event | category | flops | bytes accessed | tf_op | source)
XLA Modules:
  0.0 1517.2 jit_solution(5419906882155847757)
XLA Ops:
  7.2 1.2 fusion.28
  8.4 1.3 collective-permute-start.1
  9.7 4.5 collective-permute-start
  14.3 0.7 copy.19
  15.6 3.7 slice_bitcast_fusion.2
  20.5 0.6 convolution_add_fusion.4
  21.9 2.1 collective-permute-start.2
  24.1 1.3 collective-permute-start.3
  25.9 3.7 collective-permute-done.3
  30.1 0.6 convolution_add_fusion.3
  30.7 0.6 copy-done
  31.7 4.9 collective-permute-start.4
  36.7 1.3 collective-permute-start.5
  38.6 3.7 collective-permute-done.5
  42.8 0.6 convolution_add_fusion.2
  44.3 0.6 fusion.214
  44.9 1.3 collective-permute-start.6
  46.2 2.2 copy.20
  48.4 5.8 collective-permute-start.7
  54.3 0.8 fusion.124
  55.1 0.8 fusion.121
  55.9 0.8 fusion.161
  57.2 0.6 fusion.4
  58.3 1.3 fusion.13
  59.6 1.3 collective-permute-start.8
  60.9 2.2 copy.21
  63.2 4.7 collective-permute-start.9
  68.3 0.8 collective-permute-done.9
  69.7 0.6 fusion.5
  70.7 1.3 fusion.14
  72.0 0.6 fusion.212
  72.6 1.3 collective-permute-start.10
  73.9 1.4 copy.22
  75.3 5.1 collective-permute-start.11
  80.4 0.8 fusion.52
  81.3 0.8 fusion.49
  82.1 0.8 fusion.153
  83.4 0.7 fusion.6
  84.1 1.3 collective-permute-start.12
  85.4 2.1 collective-permute-done.12
  87.6 1.5 convert_reduce_fusion
  89.1 2.3 fusion.199
  91.4 4.1 collective-permute-start.14
  95.5 1.3 collective-permute-start.13
  97.3 5.1 collective-permute-done.13
  103.4 0.7 add_convert_fusion.1
  105.1 0.7 fusion.198
  105.8 1.3 collective-permute-start.15
  107.6 6.2 collective-permute-start.16
  114.2 0.9 collective-permute-done.16
  115.6 0.7 add_convert_fusion
  117.4 0.7 fusion.197
  118.7 3.3 select_maximum_fusion
  122.1 728.6 %reduce-scatter.2.cloned.1.call-done = f32[56,256]{1,0:T(8,128)} async-done(((f32[7168,256]{1,0:T(8,128)}), f32[56,256]{1,0:T(8,128)}) %reduce-scatter.2.cloned.1.call-update) | async-done | bytes 57360 | tf_op jit(solution)/shard_map/reduce_scatter | solution.py:182
  850.7 1.4 convert_element_type.154
  852.1 1.3 collective-permute-start.17
  853.5 4.7 collective-permute-start.18
  858.6 0.8 collective-permute-done.18
  859.9 1.4 fusion.19
  861.3 641.2 %all-gather.2.cloned.1.call-done = bf16[7168,256]{1,0:T(8,128)(2,1)} async-done(((bf16[56,256]{1,0:T(8,128)(2,1)}), bf16[7168,256]{1,0:T(8,128)(2,1)}) %all-gather.2.cloned.1.call-update) | async-done | bytes 3670032 | tf_op jit(solution)/shard_map/all_gather | solution.py:183
  1502.5 0.7 slice.610
  1503.1 0.6 broadcast_in_dim.389
  1503.7 1.9 slice.611
  1505.7 4.7 slice.609
  (247 shorter events, 14.4 us)
Async XLA Ops:
  7.2 843.5 %reduce-scatter.2.cloned.1.call-start = ((), (), s32[]{:S(2)}) async-start(), calls=%async_computation.1 | async-start | bytes 7397376 | tf_op jit(solution)/shard_map/reduce_scatter | solution.py:182
  8.4 11.6 collective-permute-start.1
  9.7 9.6 collective-permute-start
  15.4 10.4 copy-start.28
  15.4 22.7 %copy-start.51 = (pred[512]{0:T(512)(128)(4,1)}, pred[512]{0:T(512)(128)(4,1)S(1)}, u32[]{:S(2)}) copy-start(pred[512]{0:T(512)(128)(4,1)S(1)} %get-tuple-element.41) | copy-start | bytes 1540
  15.4 27.1 %copy-start.54 = (pred[512]{0:T(512)(128)(4,1)}, pred[512]{0:T(512)(128)(4,1)S(1)}, u32[]{:S(2)}) copy-start(pred[512]{0:T(512)(128)(4,1)S(1)} %get-tuple-element.37) | copy-start | bytes 1540
  15.5 10.1 copy-start.34
  15.5 14.1 copy-start.21
  15.5 14.2 copy-start.37
  15.5 22.7 %copy-start.40 = (pred[512]{0:T(512)(128)(4,1)}, pred[512]{0:T(512)(128)(4,1)S(1)}, u32[]{:S(2)}) copy-start(pred[512]{0:T(512)(128)(4,1)S(1)} %get-tuple-element.29) | copy-start | bytes 1540
  15.5 22.9 %copy-start.23 = (pred[512]{0:T(512)(128)(4,1)}, pred[512]{0:T(512)(128)(4,1)S(1)}, u32[]{:S(2)}) copy-start(pred[512]{0:T(512)(128)(4,1)S(1)} %get-tuple-element.33) | copy-start | bytes 1540
  15.6 26.8 %copy-start.26 = (pred[512]{0:T(512)(128)(4,1)}, pred[512]{0:T(512)(128)(4,1)S(1)}, u32[]{:S(2)}) copy-start(pred[512]{0:T(512)(128)(4,1)S(1)} %get-tuple-element.30) | copy-start | bytes 1540
  15.6 27.1 %copy-start.43 = (pred[512]{0:T(512)(128)(4,1)}, pred[512]{0:T(512)(128)(4,1)S(1)}, u32[]{:S(2)}) copy-start(pred[512]{0:T(512)(128)(4,1)S(1)} %get-tuple-element.28) | copy-start | bytes 1540
  21.9 9.4 copy-start.11
  21.9 3.5 collective-permute-start.2
  24.1 5.5 collective-permute-start.3
  31.3 7.3 copy-start.14
  31.7 25.5 %copy-start.17 = (f32[512,256]{1,0:T(8,128)}, f32[512,256]{1,0:T(8,128)S(1)}, u32[]{:S(2)}) copy-start(f32[512,256]{1,0:T(8,128)S(1)} %get-tuple-element.48) | copy-start | bytes 1572868
  31.7 6.4 collective-permute-start.4
  36.7 5.6 collective-permute-start.5
  44.9 9.3 collective-permute-start.6
  48.4 8.3 copy-start.24
  48.4 8.5 copy-start.41
  48.4 8.6 copy-start.52
  48.4 8.8 copy-start.9
  48.4 8.8 copy-start.58
  48.4 8.3 collective-permute-start.7
  58.3 9.6 copy-start.27
  58.3 9.7 copy-start.38
  58.3 9.9 copy-start.22
  59.6 8.3 collective-permute-start.8
  60.9 8.3 copy-start.29
  60.9 8.4 copy-start.35
  63.2 6.0 collective-permute-start.9
  72.6 7.9 collective-permute-start.10
  75.3 7.7 copy-start.49
  75.3 7.8 copy-start.46
  75.3 8.1 copy-start.4
  75.3 8.1 copy-start.5
  75.3 8.1 copy-start.73
  75.3 7.7 collective-permute-start.11
  84.1 7.3 copy-start.60
  84.1 3.4 collective-permute-start.12
  87.6 9.2 copy-start.62
  89.1 7.7 copy-start.59
  89.1 7.7 copy-start.68
  89.1 13.3 copy-start.44
  91.4 11.1 copy-start.55
  91.4 11.4 collective-permute-start.14
  95.5 7.5 copy-start.42
  95.5 6.8 collective-permute-start.13
  105.8 8.1 copy-start.39
  105.8 9.4 copy-start.36
  105.8 7.9 collective-permute-start.15
  107.6 8.0 copy-start.8
  107.6 8.0 copy-start.13
  107.6 7.5 collective-permute-start.16
  122.0 736.3 %copy-start.33 = (pred[512]{0:T(512)(128)(4,1)S(1)}, pred[512]{0:T(512)(128)(4,1)}, u32[]{:S(2)}) copy-start(pred[512]{0:T(512)(128)(4,1)} %copy-done.32) | copy-start | bytes 1540
  122.0 736.4 %copy-start.31 = (pred[512]{0:T(512)(128)(4,1)S(1)}, pred[512]{0:T(512)(128)(4,1)}, u32[]{:S(2)}) copy-start(pred[512]{0:T(512)(128)(4,1)} %copy-done.30) | copy-start | bytes 1540
  122.0 737.4 %copy-start.50 = (pred[512]{0:T(512)(128)(4,1)S(1)}, pred[512]{0:T(512)(128)(4,1)}, u32[]{:S(2)}) copy-start(pred[512]{0:T(512)(128)(4,1)} %copy-done.48) | copy-start | bytes 1540
  122.0 737.5 %copy-start.47 = (pred[512]{0:T(512)(128)(4,1)S(1)}, pred[512]{0:T(512)(128)(4,1)}, u32[]{:S(2)}) copy-start(pred[512]{0:T(512)(128)(4,1)} %copy-done.45) | copy-start | bytes 1540
  122.0 1380.4 %all-gather.2.cloned.1.call-start = ((), (), s32[]{:S(2)}) async-start(), calls=%async_computation.2 | async-start | bytes 3698688 | tf_op jit(solution)/shard_map/all_gather | solution.py:183
  852.1 6.0 collective-permute-start.17
  853.5 6.0 collective-permute-start.18
  (32 other events, 112.3 us)
Sparse Core Ops, SparseCore 0:
  122.1 728.4 reduce-scatter.1
  853.0 649.4 all-gather.1
where the time goes:
time: 1520 us
  waiting for transfers between devices  1390 us (91%)
  starting transfers between devices  55.1 us (4%)
  local copies, waits for them, and re-layouts  23.3 us (2%)
  other arithmetic  18.5 us (1%)
  matrix products  17.3 us (1%)
  between operations  15.9 us (1%)
    reduce_scatter x1, waiting for transfers between devices, shards(): lax.psum_scatter(packed, ('dp', 'seq'), scatter_dimension=0, tiled=True)  729 us
    all_gather x1, waiting for transfers between devices, shards(): lax.all_gather(packed.astype(jnp.bfloat16), ('dp', 'seq'), axis=0, tiled=...  641 us
    ppermute x9, starting transfers between devices, with_halo(): lax.ppermute(tail, axis, [(i, (i + 1) % count) for i in range(ends)])  42.1 us
  transfers between devices with their start and end apart: 21, of which 10 were waited for; matrix products, arithmetic and copies ran while one was open for 1% of the time, Pallas kernels for 0%

commit v1 on v0

--- a/solution.py
+++ b/solution.py
@@ -180,9 +180,15 @@
     share = -(-rows // (group * 8)) * 8
     packed = jnp.pad(packed, ((0, share * group - rows), (0, 0)))
     packed = lax.psum_scatter(packed, ("dp", "seq"), scatter_dimension=0, tiled=True)
-    packed = lax.all_gather(packed.astype(jnp.bfloat16), ("dp", "seq"), axis=0, tiled=True).astype(
-        jnp.float32
-    )
+    packed = jnp.concatenate(
+        lax.all_to_all(
+            jnp.stack([packed.astype(jnp.bfloat16)] * lax.axis_size(("dp", "seq"))),
+            ("dp", "seq"),
+            0,
+            0,
+        ),
+        axis=0,
+    ).astype(jnp.float32)
     total_a = packed[:rows_a].reshape(UNITS, KERNEL, channels, inner)
     total_b = packed[rows_a : rows_a + rows_b].reshape(UNITS, inner, channels)
     total_bias = packed[rows_a + rows_b : rows_a + rows_b + UNITS]

time: 1520 us -> 929 us (0.61)
  waiting for transfers between devices: 1390 us -> 787 us
    all_gather x1 -> x0, waiting for transfers between devices: 641 us -> none  [shards(): lax.all_gather(packed.astype(jnp.bfloat16), ('dp', 'seq'), axis=0, tiled=...]
    ppermute x9, waiting for transfers between devices: 12.5 us -> 43.4 us  [with_halo(): lax.ppermute(head, axis, [((i + 1) % count, i) for i in range(ends)])]
  transfers between devices with their start and end apart: 21 -> 21, of which waited for: 10 -> 10; matrix products, arithmetic and copies ran while one was open for 1% -> 2% of each run, Pallas kernels for 0% -> 0%
where the time goes in v1:
time: 929 us; the launch traced here: 927 us
  waiting for transfers between devices  787 us (85%)
  starting transfers between devices  62.9 us (7%)
  local copies, waits for them, and re-layouts  23.7 us (3%)
  other arithmetic  20.5 us (2%)
  matrix products  17.3 us (2%)
  between operations  15.9 us (2%)
    reduce_scatter x1, waiting for transfers between devices, shards(): lax.psum_scatter(packed, ('dp', 'seq'), scatter_dimension=0, tiled=True)  733 us
    ppermute x9, waiting for transfers between devices, with_halo(): lax.ppermute(head, axis, [((i + 1) % count, i) for i in range(ends)])  43.4 us
    ppermute x9, starting transfers between devices, with_halo(): lax.ppermute(tail, axis, [(i, (i + 1) % count) for i in range(ends)])  42.5 us
  transfers between devices with their start and end apart: 21, of which 10 were waited for; matrix products, arithmetic and copies ran while one was open for 2% of the time, Pallas kernels for 0%

profile of v1, /device:TPU:0, one launch (start us, length us, event | category | flops | bytes accessed | tf_op | source)
XLA Modules:
  0.0 927.2 jit_solution(17136986715719548265)
XLA Ops:
  7.2 1.2 fusion.28
  8.4 2.1 collective-permute-start
  10.5 1.3 collective-permute-start.1
  11.8 0.7 copy.19
  13.2 3.7 slice_bitcast_fusion.2
  18.0 0.6 convolution_add_fusion.4
  19.5 4.5 collective-permute-start.2
  24.1 1.3 collective-permute-start.3
  25.9 3.7 collective-permute-done.3
  30.1 0.6 convolution_add_fusion.3
  31.7 4.8 collective-permute-start.4
  36.6 1.3 collective-permute-start.5
  38.5 4.9 collective-permute-done.5
  43.9 0.6 convolution_add_fusion.2
  45.4 0.6 fusion.214
  46.0 1.3 collective-permute-start.6
  47.3 2.2 copy.20
  49.6 5.9 collective-permute-start.7
  55.5 0.8 fusion.124
  56.3 0.8 fusion.121
  57.1 0.8 fusion.161
  58.4 0.6 fusion.4
  59.5 1.3 fusion.13
  60.8 1.3 collective-permute-start.8
  62.1 2.2 copy.21
  64.4 4.7 collective-permute-start.9
  69.6 0.8 collective-permute-done.9
  70.9 0.6 fusion.5
  71.9 1.3 fusion.14
  73.2 0.6 fusion.212
  73.8 1.3 collective-permute-start.10
  75.1 1.4 copy.22
  76.6 5.1 collective-permute-start.11
  81.7 0.8 fusion.52
  82.5 0.8 fusion.49
  83.4 0.8 fusion.153
  84.7 0.7 fusion.6
  85.4 1.3 collective-permute-start.12
  86.7 2.1 collective-permute-done.12
  88.8 1.5 convert_reduce_fusion
  90.4 2.3 fusion.199
  92.7 1.3 collective-permute-start.13
  94.0 4.7 collective-permute-start.14
  100.6 0.7 add_convert_fusion.1
  102.4 0.7 fusion.198
  103.1 1.3 collective-permute-start.15
  104.9 5.9 collective-permute-start.16
  111.3 0.9 collective-permute-done.16
  112.6 0.7 add_convert_fusion
  114.4 0.7 fusion.197
  115.7 3.2 select_maximum_fusion
  119.0 732.7 %reduce-scatter.2.cloned.1.call-done = f32[56,256]{1,0:T(8,128)} async-done(((f32[7168,256]{1,0:T(8,128)}), f32[56,256]{1,0:T(8,128)}) %reduce-scatter.2.cloned.1.call-update) | async-done | bytes 57360 | tf_op jit(solution)/shard_map/reduce_scatter | solution.py:182
  851.7 0.8 convert_element_type.157
  852.5 2.1 stack.29
  854.6 7.4 all-to-all-start
  862.1 1.3 collective-permute-start.17
  863.4 4.7 collective-permute-start.18
  868.1 34.7 %collective-permute-done.17 = bf16[3,256]{1,0:T(4,128)(2,1)S(1)} collective-permute-done((bf16[3,256]{1,0:T(4,128)(2,1)S(1)}, bf16[3,256]{1,0:T(4,128)(2,1)S(1)}, u32[]{:S(2)}, u32[]{:S(2)}) %collective-permute-start.17) | collective-permute-done | bytes 1568 | tf_op jit(solution)/shard_map/ppermute | solution.py:20
  903.8 1.4 fusion.19
  905.2 6.3 all-to-all-done
  911.6 2.6 convert_element_type.158
  914.2 0.9 slice.612
  915.1 0.6 broadcast_in_dim.389
  915.7 4.7 slice.610
  (252 shorter events, 15.3 us)
Async XLA Ops:
  7.2 844.6 %reduce-scatter.2.cloned.1.call-start = ((), (), s32[]{:S(2)}) async-start(), calls=%async_computation.2 | async-start | bytes 7397376 | tf_op jit(solution)/shard_map/reduce_scatter | solution.py:182
  8.4 8.5 collective-permute-start
  10.5 7.0 collective-permute-start.1
  12.9 12.8 %copy-start.28 = (pred[512]{0:T(512)(128)(4,1)}, pred[512]{0:T(512)(128)(4,1)S(1)}, u32[]{:S(2)}) copy-start(pred[512]{0:T(512)(128)(4,1)S(1)} %get-tuple-element.40) | copy-start | bytes 1540
  12.9 25.1 %copy-start.51 = (pred[512]{0:T(512)(128)(4,1)}, pred[512]{0:T(512)(128)(4,1)S(1)}, u32[]{:S(2)}) copy-start(pred[512]{0:T(512)(128)(4,1)S(1)} %get-tuple-element.41) | copy-start | bytes 1540
  13.0 30.6 %copy-start.54 = (pred[512]{0:T(512)(128)(4,1)}, pred[512]{0:T(512)(128)(4,1)S(1)}, u32[]{:S(2)}) copy-start(pred[512]{0:T(512)(128)(4,1)S(1)} %get-tuple-element.37) | copy-start | bytes 1540
  13.1 12.5 %copy-start.34 = (pred[512]{0:T(512)(128)(4,1)}, pred[512]{0:T(512)(128)(4,1)S(1)}, u32[]{:S(2)}) copy-start(pred[512]{0:T(512)(128)(4,1)S(1)} %get-tuple-element.32) | copy-start | bytes 1540
  13.1 16.5 %copy-start.21 = (pred[512]{0:T(512)(128)(4,1)}, pred[512]{0:T(512)(128)(4,1)S(1)}, u32[]{:S(2)}) copy-start(pred[512]{0:T(512)(128)(4,1)S(1)} %get-tuple-element.34) | copy-start | bytes 1540
  13.1 16.7 %copy-start.37 = (pred[512]{0:T(512)(128)(4,1)}, pred[512]{0:T(512)(128)(4,1)S(1)}, u32[]{:S(2)}) copy-start(pred[512]{0:T(512)(128)(4,1)S(1)} %get-tuple-element.31) | copy-start | bytes 1540
  13.1 25.1 %copy-start.40 = (pred[512]{0:T(512)(128)(4,1)}, pred[512]{0:T(512)(128)(4,1)S(1)}, u32[]{:S(2)}) copy-start(pred[512]{0:T(512)(128)(4,1)S(1)} %get-tuple-element.29) | copy-start | bytes 1540
  13.1 25.2 %copy-start.23 = (pred[512]{0:T(512)(128)(4,1)}, pred[512]{0:T(512)(128)(4,1)S(1)}, u32[]{:S(2)}) copy-start(pred[512]{0:T(512)(128)(4,1)S(1)} %get-tuple-element.33) | copy-start | bytes 1540
  13.1 30.3 %copy-start.26 = (pred[512]{0:T(512)(128)(4,1)}, pred[512]{0:T(512)(128)(4,1)S(1)}, u32[]{:S(2)}) copy-start(pred[512]{0:T(512)(128)(4,1)S(1)} %get-tuple-element.30) | copy-start | bytes 1540
  13.1 30.6 %copy-start.43 = (pred[512]{0:T(512)(128)(4,1)}, pred[512]{0:T(512)(128)(4,1)S(1)}, u32[]{:S(2)}) copy-start(pred[512]{0:T(512)(128)(4,1)S(1)} %get-tuple-element.28) | copy-start | bytes 1540
  19.5 11.8 %copy-start.11 = (f32[512,256]{1,0:T(8,128)}, f32[512,256]{1,0:T(8,128)S(1)}, u32[]{:S(2)}) copy-start(f32[512,256]{1,0:T(8,128)S(1)} %get-tuple-element.46) | copy-start | bytes 1572868
  19.5 5.9 collective-permute-start.2
  24.1 5.5 collective-permute-start.3
  31.7 26.7 %copy-start.17 = (f32[512,256]{1,0:T(8,128)}, f32[512,256]{1,0:T(8,128)S(1)}, u32[]{:S(2)}) copy-start(f32[512,256]{1,0:T(8,128)S(1)} %get-tuple-element.48) | copy-start | bytes 1572868
  31.7 6.3 collective-permute-start.4
  36.6 6.8 collective-permute-start.5
  46.0 9.4 %collective-permute-start.6 = (bf16[27,256]{1,0:T(8,128)(2,1)}, bf16[27,256]{1,0:T(8,128)(2,1)S(1)}, u32[]{:S(2)}, u32[]{:S(2)}) collective-permute-start(bf16[27,256]{1,0:T(8,128)(2,1)} %get-tuple-element.21), channel_id=1, source_target_pairs={{2,0},{4,2},{6,4},{8,6},{10,8},{12,10},{14,12},{16,14},{18,16},{20... | collective-permute-start | bytes 41480 | tf_op jit(solution)/shard_map/ppermute | solution.py:20
  49.6 8.4 copy-start.24
  49.6 8.5 copy-start.41
  49.6 8.7 copy-start.52
  49.6 8.9 copy-start.9
  49.6 8.9 copy-start.58
  49.6 8.4 collective-permute-start.7
  59.5 9.6 %copy-start.27 = (pred[512]{0:T(512)(128)(4,1)S(1)}, pred[512]{0:T(512)(128)(4,1)}, u32[]{:S(2)}) copy-start(pred[512]{0:T(512)(128)(4,1)} %copy-done.26) | copy-start | bytes 1540
  59.5 9.8 %copy-start.38 = (pred[512]{0:T(512)(128)(4,1)S(1)}, pred[512]{0:T(512)(128)(4,1)}, u32[]{:S(2)}) copy-start(pred[512]{0:T(512)(128)(4,1)} %copy-done.37) | copy-start | bytes 1540
  59.5 9.9 %copy-start.22 = (pred[512]{0:T(512)(128)(4,1)S(1)}, pred[512]{0:T(512)(128)(4,1)}, u32[]{:S(2)}) copy-start(pred[512]{0:T(512)(128)(4,1)} %copy-done.21) | copy-start | bytes 1540
  60.8 8.3 collective-permute-start.8
  62.1 8.3 copy-start.29
  62.1 8.5 copy-start.35
  64.4 6.0 collective-permute-start.9
  73.8 7.9 collective-permute-start.10
  76.6 7.7 copy-start.49
  76.6 7.8 copy-start.46
  76.6 8.1 copy-start.4
  76.6 8.1 copy-start.5
  76.6 8.1 copy-start.70
  76.6 7.7 collective-permute-start.11
  85.4 7.3 copy-start.60
  85.4 3.4 collective-permute-start.12
  88.8 9.9 %copy-start.62 = (bf16[512,256]{1,0:T(8,128)(2,1)}, bf16[512,256]{1,0:T(8,128)(2,1)S(1)}, u32[]{:S(2)}) copy-start(bf16[512,256]{1,0:T(8,128)(2,1)S(1)} %collective-permute-done.12) | copy-start | bytes 786436
  90.4 8.3 copy-start.59
  90.4 8.3 copy-start.68
  90.4 8.8 copy-start.44
  92.7 6.5 collective-permute-start.13
  94.0 6.1 collective-permute-start.14
  103.1 7.8 copy-start.39
  103.1 9.2 copy-start.36
  103.1 7.7 collective-permute-start.15
  104.9 7.7 copy-start.8
  104.9 7.7 copy-start.13
  104.9 7.3 collective-permute-start.16
  854.6 48.4 %copy-start.33 = (pred[512]{0:T(512)(128)(4,1)S(1)}, pred[512]{0:T(512)(128)(4,1)}, u32[]{:S(2)}) copy-start(pred[512]{0:T(512)(128)(4,1)} %copy-done.32) | copy-start | bytes 1540
  854.6 48.5 %copy-start.31 = (pred[512]{0:T(512)(128)(4,1)S(1)}, pred[512]{0:T(512)(128)(4,1)}, u32[]{:S(2)}) copy-start(pred[512]{0:T(512)(128)(4,1)} %copy-done.30) | copy-start | bytes 1540
  854.6 57.0 %all-to-all-start = ((bf16[128,56,256]{2,1,0:T(8,128)(2,1)}), bf16[128,56,256]{2,1,0:T(8,128)(2,1)}, u32[]{:S(2)}, u32[]{:S(2)}) async-start(bf16[128,56,256]{2,1,0:T(8,128)(2,1)} %stack.29), calls=%async_computation.1 | async-start | bytes 7340032 | tf_op jit(solution)/shard_map/all_to_all | solution.py:184
  862.1 41.3 %copy-start.50 = (pred[512]{0:T(512)(128)(4,1)S(1)}, pred[512]{0:T(512)(128)(4,1)}, u32[]{:S(2)}) copy-start(pred[512]{0:T(512)(128)(4,1)} %copy-done.48) | copy-start | bytes 1540
  862.1 41.4 %copy-start.47 = (pred[512]{0:T(512)(128)(4,1)S(1)}, pred[512]{0:T(512)(128)(4,1)}, u32[]{:S(2)}) copy-start(pred[512]{0:T(512)(128)(4,1)} %copy-done.45) | copy-start | bytes 1540
  862.1 40.7 %collective-permute-start.17 = (bf16[3,256]{1,0:T(4,128)(2,1)S(1)}, bf16[3,256]{1,0:T(4,128)(2,1)S(1)}, u32[]{:S(2)}, u32[]{:S(2)}) collective-permute-start(bf16[3,256]{1,0:T(4,128)(2,1)S(1)} %get-tuple-element.11), channel_id=1, source_target_pairs={{2,0},{4,2},{6,4},{8,6},{10,8},{12,10},{14,12},{16,14},{18,16},{20... | collective-permute-start | bytes 4616 | tf_op jit(solution)/shard_map/ppermute | solution.py:20
  863.4 40.4 %copy-start.6 = (bf16[7,256,256]{2,1,0:T(8,128)(2,1)S(1)}, bf16[7,256,256]{2,1,0:T(8,128)(2,1)}, u32[]{:S(2)}) copy-start(bf16[7,256,256]{2,1,0:T(8,128)(2,1)} %copy.22) | copy-start | bytes 2752516
  863.4 40.4 %copy-start.61 = (bf16[512,256]{1,0:T(8,128)(2,1)S(1)}, bf16[512,256]{1,0:T(8,128)(2,1)}, u32[]{:S(2)}) copy-start(bf16[512,256]{1,0:T(8,128)(2,1)} %copy-done.60) | copy-start | bytes 786436
  863.4 40.4 %copy-start.76 = (bf16[512,256]{1,0:T(8,128)(2,1)S(1)}, bf16[512,256]{1,0:T(8,128)(2,1)}, u32[]{:S(2)}) copy-start(bf16[512,256]{1,0:T(8,128)(2,1)} %copy-done.75) | copy-start | bytes 786436
  863.4 39.9 %collective-permute-start.18 = (bf16[3,256]{1,0:T(4,128)(2,1)S(1)}, bf16[3,256]{1,0:T(4,128)(2,1)S(1)}, u32[]{:S(2)}, u32[]{:S(2)}) collective-permute-start(bf16[3,256]{1,0:T(4,128)(2,1)S(1)} %get-tuple-element.10), channel_id=1, source_target_pairs={{0,2},{2,4},{4,6},{6,8},{8,10},{10,12},{12,14},{14,16},{16,18},{18... | collective-permute-start | bytes 4616 | tf_op jit(solution)/shard_map/ppermute | solution.py:18
  (34 other events, 105.3 us)
Sparse Core Ops, SparseCore 0:
  119.1 732.5 reduce-scatter.1
